TPU v7x, 32 devices: a whole 2x2x4 slice. The times are simulated.
32 devices in a mesh: req: 8 (over z, y), tp: 4 (over x, core).
Axes of the slice: x: 2, y: 2, z: 4, core: 2. Of those that a mesh axis runs over, the one named last changes fastest.
Arguments:
- hidden_in: bfloat16 [192, 1536], P('req', 'tp'), may hold values from -12 to 12
- queries: bfloat16 [192, 1536], P('req', 'tp'), may hold values from -6 to 6
- fresh_key_value: bfloat16 [192, 2, 256], P('req'), may hold values from -120 to 120
- positions: int32 [192], P('req'), may hold values from 0 to 4095
- lengths: int32 [8, 24], P('req'), may hold values from 1 to 2048, 3072 in all within a row
- cache: bfloat16 [24576, 2, 2, 128], P(('req', 'tp')), may hold values from -160 to 160
- out_proj: bfloat16 [1536, 1536], P('tp'), may hold values from -0.59765625 to 0.59765625
- norm_gain: float32 [1536], replicated, may hold values from 0.1 to 1.9
- expert_ids: int32 [192, 4], P('req'), may hold values from 0 to 31, all different within a row; in each aligned block of 24 rows (0 to 23, 24 to 47, ...) at most 8 rows name the same one
- router_weights: float32 [192, 4], P('req'), may hold values from 0.05 to 0.5
- gate_up: bfloat16 [32, 2, 1536, 768], P('req', None, None, 'tp'), may hold values from -0.15625 to 0.15625
- down: bfloat16 [32, 768, 1536], P('req', 'tp'), may hold values from -0.21875 to 0.21875
Outputs:
- layer_out: bfloat16 [192, 1536], P('req', 'tp')
Inputs may be any that keep to these rules, and one draw needn't show every extreme that they name: `lengths`: each row sums to 3072. `expert_ids`: each row names 4 different experts; among the 24 aligned rows of one request group no expert is named by more than 8 rows, a bound that some block reaches.
All inputs are finite; a program needn't handle non-finite values.
Results may differ from a plain program's by a relative error of at most 0.012.
The roundings to bfloat16 on the way count: a program that leaves them out, or rounds other values in their place, can miss the bound.
Values may be sent and summed in bfloat16 or wider, within the bound.
No kernel may reach another device: no remote copies, remote signals or barrier semaphores. Data moves between devices by JAX's collectives and lax.ppermute only.
A program may use at most 64 MiB of HBM per device.

v0:
```python
import jax
import jax.numpy as jnp
from jax import lax
from jax.sharding import PartitionSpec as P

EXPERTS = 32
rope_base = 1000000.0
norm_eps = 1e-06
neg_floor = -1e30


def apply_rotary_heads(values, positions, head_size):
    half_size = head_size // 2
    exponents = jnp.arange(half_size, dtype=jnp.float32) * (2.0 / head_size)
    inverse_freq = jnp.power(jnp.float32(rope_base), -exponents)
    angles = positions.astype(jnp.float32)[:, None] * inverse_freq[None, :]
    cosine = jnp.cos(angles)[:, None, :]
    sine = jnp.sin(angles)[:, None, :]
    first_half = values[..., :half_size]
    second_half = values[..., half_size:]
    return jnp.concatenate(
        [first_half * cosine - second_half * sine, second_half * cosine + first_half * sine],
        axis=-1,
    )


def per_device(
    hidden_in,
    queries,
    fresh_key_value,
    positions,
    lengths,
    cache,
    out_proj,
    norm_gain,
    expert_ids,
    router_weights,
    gate_up,
    down,
):
    tp_count = lax.axis_size("tp")
    req_count = lax.axis_size("req")
    tp_index = lax.axis_index("tp")
    req_index = lax.axis_index("req")
    row_count = hidden_in.shape[0]
    head_size = cache.shape[3]
    kv_count = cache.shape[2]
    own_heads = queries.shape[1] // head_size
    head_count = own_heads * tp_count
    request_group_size = head_count // kv_count
    score_scaling = head_size ** (-0.5)
    model_width = norm_gain.shape[0]
    own_width = hidden_in.shape[1]
    first_head = tp_index * own_heads
    span_rows = cache.shape[0]
    q_local = apply_rotary_heads(
        queries.reshape(row_count, own_heads, head_size).astype(jnp.float32), positions, head_size
    ).astype(jnp.bfloat16)
    packed = jnp.stack([q_local.reshape(row_count, own_width), hidden_in], axis=0)
    gathered = lax.all_gather(packed, "tp", axis=0)
    q_all = jnp.transpose(gathered[:, 0], (1, 0, 2)).reshape(
        row_count, kv_count, request_group_size, head_size
    )
    hidden_full = jnp.transpose(gathered[:, 1], (1, 0, 2)).reshape(row_count, model_width)
    k_new = apply_rotary_heads(
        fresh_key_value[:, 0].reshape(row_count, kv_count, head_size).astype(jnp.float32),
        positions,
        head_size,
    ).astype(jnp.bfloat16)
    value_fresh = fresh_key_value[:, 1].reshape(row_count, kv_count, head_size)
    own_score = (
        jnp.einsum("rcgd,rcd->rcg", q_all, k_new, preferred_element_type=jnp.float32)
        * score_scaling
    )
    segment_ends = jnp.cumsum(lengths[0], dtype=jnp.int32)
    segment_starts = segment_ends - lengths[0]
    cache_spots = tp_index * span_rows + jnp.arange(span_rows, dtype=jnp.int32)
    mask = (cache_spots[None, :] >= segment_starts[:, None]) & (
        cache_spots[None, :] < segment_ends[:, None]
    )
    mask = mask[:, None, None, :]
    keys = cache[:, 0]
    values = cache[:, 1]
    scores = (
        jnp.einsum("rcgd,jcd->rcgj", q_all, keys, preferred_element_type=jnp.float32)
        * score_scaling
    )
    scores = jnp.where(mask, scores, neg_floor)
    highest_local = jnp.max(scores, axis=3)
    weights = jnp.where(mask, jnp.exp(scores - highest_local[..., None]), 0.0)
    totals_local = jnp.sum(weights, axis=3)
    sums_local = jnp.einsum(
        "rcgj,jcd->rcgd",
        weights,
        values.astype(jnp.float32),
        precision=lax.Precision.HIGHEST,
        preferred_element_type=jnp.float32,
    )
    states = jnp.concatenate(
        [highest_local[..., None], totals_local[..., None], sums_local], axis=3
    ).reshape(row_count, head_count, head_size + 2)
    all_states = lax.all_gather(states, "tp", axis=0)
    all_states = lax.dynamic_slice_in_dim(all_states, first_head, own_heads, 2)
    parts_highest = all_states[..., 0]
    parts_totals = all_states[..., 1]
    parts_sums = all_states[..., 2:]
    own_slice = lax.dynamic_slice_in_dim(
        own_score.reshape(row_count, head_count), first_head, own_heads, 1
    )
    top_score = jnp.maximum(jnp.max(parts_highest, axis=0), own_slice)
    factors = jnp.exp(parts_highest - top_score[None])
    own_part = jnp.exp(own_slice - top_score)
    head_kv = (first_head + jnp.arange(own_heads, dtype=jnp.int32)) // request_group_size
    own_values = jnp.take(value_fresh, head_kv, axis=1).astype(jnp.float32)
    totals = jnp.sum(parts_totals * factors, axis=0) + own_part
    summed = jnp.sum(parts_sums * factors[..., None], axis=0) + own_values * own_part[..., None]
    attention_output = (
        (summed / totals[..., None]).astype(jnp.bfloat16).reshape(row_count, own_heads * head_size)
    )
    partial_proj = jnp.dot(attention_output, out_proj, preferred_element_type=jnp.float32)
    projected = lax.psum(partial_proj, "tp")
    residual = hidden_full.astype(jnp.float32) + projected
    mean_square = jnp.mean(residual * residual, axis=1, keepdims=True)
    normed = (residual * lax.rsqrt(mean_square + norm_eps) * norm_gain[None, :]).astype(
        jnp.bfloat16
    )
    local_count = gate_up.shape[0]
    block_total = local_count * req_count
    split_count = max(1, block_total // EXPERTS)
    expert_range = jnp.arange(EXPERTS, dtype=jnp.int32)
    member = jnp.any(expert_ids[:, :, None] == expert_range[None, None, :], axis=1)
    member_int = member.astype(jnp.int32)
    slot_of = jnp.cumsum(member_int, axis=0, dtype=jnp.int32) - member_int
    slot_taken = jnp.take_along_axis(slot_of, expert_ids, axis=1)
    block_taken = slot_taken % split_count * EXPERTS + expert_ids
    block_range = jnp.arange(block_total, dtype=jnp.int32)
    block_weights = jnp.sum(
        jnp.where(
            block_taken[:, :, None] == block_range[None, None, :], router_weights[:, :, None], 0.0
        ),
        axis=1,
    )
    rows_all = lax.all_gather(normed, "req", axis=0, tiled=True)
    weights_all = lax.all_gather(block_weights, "req", axis=0, tiled=True)
    weights_own = lax.dynamic_slice_in_dim(weights_all, req_index * local_count, local_count, 1)
    mixed = jnp.zeros((rows_all.shape[0], model_width), jnp.float32)
    for local_block in range(local_count):
        gate_part = jnp.dot(rows_all, gate_up[local_block, 0], preferred_element_type=jnp.float32)
        up_part = jnp.dot(rows_all, gate_up[local_block, 1], preferred_element_type=jnp.float32)
        activation = (jnp.maximum(gate_part, 0.0) * up_part).astype(jnp.bfloat16)
        produced = jnp.dot(activation, down[local_block], preferred_element_type=jnp.float32)
        produced = produced.astype(jnp.bfloat16).astype(jnp.float32)
        mixed = mixed + weights_own[:, local_block : local_block + 1] * produced
    mixed = mixed.reshape(req_count, row_count, tp_count, own_width)
    mixed = jnp.transpose(mixed, (0, 2, 1, 3)).reshape(req_count * tp_count, row_count, own_width)
    mixed = lax.psum_scatter(mixed, ("req", "tp"), scatter_dimension=0, tiled=True)
    mixed = mixed.reshape(row_count, own_width)
    residual_own = lax.dynamic_slice_in_dim(residual, tp_index * own_width, own_width, 1)
    return (residual_own + mixed).astype(jnp.bfloat16)


def solution(mesh):
    placed = (
        P("req", "tp"),
        P("req", "tp"),
        P("req", None, None),
        P("req"),
        P("req", None),
        P(("req", "tp"), None, None, None),
        P("tp", None),
        P(),
        P("req", None),
        P("req", None),
        P("req", None, None, "tp"),
        P("req", "tp", None),
    )
    return jax.shard_map(
        per_device, mesh=mesh, in_specs=placed, out_specs=P("req", "tp"), check_vma=False
    )
```

profile of v0, /device:TPU:0, one launch (start us, length us, event | category | flops | bytes accessed | tf_op | source)
XLA Modules:
  0.0 226.4 jit_solution(6006693005743040945)
XLA Ops:
  6.6 0.8 convert_element_type.94
  7.4 0.7 reshape.253
  8.1 0.1 multiply_cosine_fusion
  8.3 0.1 subtract_convert_fusion
  8.4 0.1 pad_maximum_fusion.2
  8.5 0.7 pad_maximum_fusion.1
  9.2 6.6 %all-gather = bf16[8,24,384]{2,1,0:T(8,128)(2,1)S(1)} all-gather(bf16[2,24,384]{2,1,0:T(8,128)(2,1)S(1)} %pad_maximum_fusion.1), channel_id=2, replica_groups=mesh['req'=8,'tp'=4] {'tp'}, dimensions={0}, use_global_device_ids=true | all-gather | bytes 184320 | tf_op jit(solution)/shard_map/all_gather | solution.py:60
  16.0 0.1 copy.58
  16.1 0.1 reduce.1
  16.2 0.5 fusion.74
  16.9 0.5 fusion.76
  17.3 0.1 concatenate.24
  17.5 0.3 fusion.18
  17.8 0.7 fusion.17
  18.5 0.1 concatenate.25
  18.6 0.2 pad_maximum_fusion
  18.9 11.1 %all_gather.17 = f32[4,24,12,130]{3,1,2,0:T(8,128)S(1)} all-gather(f32[1,24,12,130]{3,1,2,0:T(8,128)S(1)} %pad_maximum_fusion), channel_id=1, replica_groups=mesh['req'=8,'tp'=4] {'tp'}, dimensions={0}, use_global_device_ids=true | all-gather | bytes 748800 | tf_op jit(solution)/shard_map/all_gather | solution.py:102
  30.0 0.1 subtract_convert_fusion.1
  30.1 0.1 maximum_bitcast_fusion
  30.2 0.2 fusion.58
  30.4 0.1 copy.75
  30.5 0.2 fusion.73
  30.7 0.1 copy.82
  30.8 0.1 constant_dynamic-slice_fusion.1
  30.9 0.3 copy.81
  31.3 0.6 multiply_reduce_fusion
  31.9 0.1 copy.66
  32.0 0.1 copy.83
  32.5 0.6 gather_fusion
  33.3 0.9 fusion.60
  34.4 0.1 select_reduce_fusion
  34.5 31.0 %all_gather.18 = f32[192,32]{1,0:T(8,128)S(1)} all-gather(f32[24,32]{1,0:T(8,128)S(1)} %select_reduce_fusion), channel_id=1, replica_groups=mesh['req'=8,'tp'=4] {'req'}, dimensions={0}, use_global_device_ids=true | all-gather | bytes 27648 | tf_op jit(solution)/shard_map/all_gather | solution.py:144
  65.4 0.4 dynamic-slice_reduce_fusion
  65.8 1.0 all-reduce.3.cloned.1.call-done
  66.8 1.0 multiply_reduce_fusion.1
  68.0 31.8 %all_gather.19 = bf16[192,1536]{1,0:T(8,128)(2,1)S(1)} all-gather(bf16[24,1536]{1,0:T(8,128)(2,1)S(1)} %multiply_convert_fusion), channel_id=1, replica_groups=mesh['req'=8,'tp'=4] {'req'}, dimensions={0}, use_global_device_ids=true | all-gather | bytes 663552 | tf_op jit(solution)/shard_map/all_gather | solution.py:143
  99.8 2.1 convolution_maximum_fusion.3
  101.9 2.1 convolution_maximum_fusion.2
  104.0 1.4 convolution_maximum_fusion.1
  105.4 1.4 convolution_maximum_fusion
  106.8 2.2 fusion.10
  109.0 3.2 %fusion.8 = f32[192,1536]{1,0:T(8,128)} fusion(f32[192,1536]{1,0:T(8,128)S(1)} %fusion.10, f32[192,192]{1,0:T(8,128)} %convolution_maximum_fusion.2, bf16[192,1536]{1,0:T(8,128)(2,1)S(1)} %all_gather.19, bf16[4,192,1536]{2,1,0:T(8,128)(2,1)} %param.23, bf16[4,2,1536,192]{2,3,1,0:T(8,128)(2,1)} %param.22, f32[192]{0:T(256)S(1)} %get-tuple-element.7), kind=kOutput, calls=%fused_computation.12 | convolution fusion | flops 227745792 | bytes 4326144 | tf_op jit(solution)/shard_map/dot_general | solution.py:151
  112.2 2.5 %fusion.5 = f32[192,1536]{1,0:T(8,128)S(1)} fusion(f32[192,1536]{1,0:T(8,128)} %fusion.8, f32[192,192]{1,0:T(8,128)S(1)} %convolution_maximum_fusion.1, bf16[192,1536]{1,0:T(8,128)(2,1)S(1)} %all_gather.19, bf16[4,192,1536]{2,1,0:T(8,128)(2,1)} %param.23, bf16[4,2,1536,192]{2,3,1,0:T(8,128)(2,1)} %param.22, f32[192]{0:T(256)S(1)} %get-tuple-element.6), kind=kOutput, calls=%fused_computation.8 | convolution fusion | flops 227745792 | bytes 4276992 | tf_op jit(solution)/shard_map/dot_general | solution.py:151
  114.7 3.1 %fusion.2 = f32[192,1536]{1,0:T(8,128)} fusion(f32[192,1536]{1,0:T(8,128)S(1)} %fusion.5, f32[192,192]{1,0:T(8,128)S(1)} %convolution_maximum_fusion, bf16[192,1536]{1,0:T(8,128)(2,1)S(1)} %all_gather.19, bf16[4,192,1536]{2,1,0:T(8,128)(2,1)} %param.23, bf16[4,2,1536,192]{2,3,1,0:T(8,128)(2,1)} %param.22, f32[192]{0:T(256)S(1)} %get-tuple-element.5), kind=kOutput, calls=%fused_computation.4 | convolution fusion | flops 227745792 | bytes 4276992 | tf_op jit(solution)/shard_map/dot_general | solution.py:151
  117.8 1.7 reshape.250
  119.5 1.1 copy.71
  120.6 97.6 %reduce-scatter.4.cloned.1.call-done = f32[1,24,384]{2,1,0:T(8,128)} async-done(((f32[32,24,384]{2,1,0:T(8,128)}), f32[1,24,384]{2,1,0:T(8,128)}) %reduce-scatter.4.cloned.1.call-update) | async-done | bytes 36880
  218.2 1.4 fusion.57
  (47 shorter events, 1.2 us)
Async XLA Ops:
  6.5 26.7 %copy-start = (bf16[384,1536]{1,0:T(8,128)(2,1)S(1)}, bf16[384,1536]{1,0:T(8,128)(2,1)}, u32[]{:S(2)}) copy-start(bf16[384,1536]{1,0:T(8,128)(2,1)} %param.18) | copy-start | bytes 3538948
  6.5 9.4 %copy-start.6 = (s32[1,24]{1,0:T(1,128)S(1)}, s32[1,24]{1,0:T(1,128)}, u32[]{:S(2)}) copy-start(s32[1,24]{1,0:T(1,128)} %param.16) | copy-start | bytes 292
  6.5 9.7 %copy-start.1 = (bf16[768,2,2,128]{3,2,1,0:T(2,128)(2,1)S(1)}, bf16[768,2,2,128]{3,2,1,0:T(2,128)(2,1)}, u32[]{:S(2)}) copy-start(bf16[768,2,2,128]{3,2,1,0:T(2,128)(2,1)} %param.17) | copy-start | bytes 2359300
  6.5 60.3 %all-reduce.3.cloned.1.call-start = ((), (), s32[]{:S(2)}) async-start(), calls=%async_computation.1 | async-start | bytes 294912 | tf_op jit(solution)/shard_map/psum | solution.py:121
  18.5 11.4 %copy-start.2 = (bf16[24,2,256]{2,1,0:T(2,128)(2,1)S(1)}, bf16[24,2,256]{2,1,0:T(2,128)(2,1)}, u32[]{:S(2)}) copy-start(bf16[24,2,256]{2,1,0:T(2,128)(2,1)} %param.14) | copy-start | bytes 73732
  33.0 1.3 copy-start.4
  33.1 1.3 copy-start.5
  34.2 33.7 %copy-start.3 = (f32[1536]{0:T(1024)S(1)}, f32[1536]{0:T(1024)}, u32[]{:S(2)}) copy-start(f32[1536]{0:T(1024)} %param.19) | copy-start | bytes 18436
  34.2 184.0 %reduce-scatter.4.cloned.1.call-start = ((), (), s32[]{:S(2)}) async-start(), calls=%async_computation.2 | async-start | bytes 1216512
Sparse Core Ops, SparseCore 0:
  34.3 32.4 all-reduce.2
  120.7 97.4 reduce-scatter.3
where the time goes:
time: 227 us; the launch traced here: 226 us
  waiting for transfers between devices  98.7 us (43%)
  blocking collectives  80.5 us (35%)
  matrix products  20.2 us (9%)
  between operations  13.8 us (6%)
  local copies, waits for them, and re-layouts  6.85 us (3%)
  other arithmetic  6.41 us (3%)
    unnamed x3, waiting for transfers between devices  97.7 us
    all_gather x1, blocking collectives, per_device(): rows_all = lax.all_gather(normed, 'req', axis=0, tiled=True)  31.8 us
    all_gather x1, blocking collectives, per_device(): weights_all = lax.all_gather(block_weights, 'req', axis=0, tiled=True)  31 us
    all_gather x1, blocking collectives, per_device(): all_states = lax.all_gather(states, 'tp', axis=0)  11.1 us
    dot_general x4, matrix products, per_device(): jnp.dot(activation, down[local_block], preferred_element_type=jnp.float32)  11 us
    dot_general x4, matrix products, per_device(): jnp.dot(rows_all, gate_up[local_block, 0], preferred_element_type=jnp.flo...  6.93 us
    all_gather x1, blocking collectives, per_device(): gathered = lax.all_gather(packed, 'tp', axis=0)  6.58 us
  transfers between devices with their start and end apart: 2, of which 2 were waited for; matrix products, arithmetic and copies ran while one was open for 0% of the time, Pallas kernels for 0%

commit v1 on v0

--- a/solution.py
+++ b/solution.py
@@ -140,8 +140,9 @@
         ),
         axis=1,
     )
-    rows_all = lax.all_gather(normed, "req", axis=0, tiled=True)
-    weights_all = lax.all_gather(block_weights, "req", axis=0, tiled=True)
+    t1 = jnp.concatenate([normed, block_weights], 1)
+    a_now = jax.lax.all_gather(t1, "req", axis=0, tiled=True)
+    rows_all, weights_all = jnp.split(a_now, [normed.shape[1]], 1)
     weights_own = lax.dynamic_slice_in_dim(weights_all, req_index * local_count, local_count, 1)
     mixed = jnp.zeros((rows_all.shape[0], model_width), jnp.float32)
     for local_block in range(local_count):

time: 227 us -> 240 us (1.057)
  waiting for transfers between devices: 98.7 us -> 171 us
  blocking collectives: 80.5 us -> 17.7 us
    all_gather x2 -> x0, blocking collectives: 62.8 us -> none  [the longest x1 31.8 us: per_device(): rows_all = lax.all_gather(normed, 'req', axis=0, tiled=True)]
    all_gather x0 -> x1, waiting for transfers between devices: none -> 42.7 us  [per_device(): a_now = jax.lax.all_gather(t1, 'req', axis=0, tiled=True)]
    psum x1, waiting for transfers between devices: 1.03 us -> 32.4 us  [per_device(): projected = lax.psum(partial_proj, 'tp')]
    dot_general x4, matrix products: 11 us -> 13.6 us  [per_device(): jnp.dot(activation, down[local_block], preferred_element_type=jnp.float32)]
    unnamed x3 -> x4, waiting for transfers between devices: 97.7 us -> 96.1 us
  transfers between devices with their start and end apart: 2 -> 3, of which waited for: 2 -> 3; matrix products, arithmetic and copies ran while one was open for 0% -> 0% of each run, Pallas kernels for 0% -> 0%
where the time goes in v1:
time: 240 us; the launch traced here: 239 us
  waiting for transfers between devices  171 us (71%)
  matrix products  21.8 us (9%)
  blocking collectives  17.7 us (7%)
  between operations  13.5 us (6%)
  local copies, waits for them, and re-layouts  7.83 us (3%)
  other arithmetic  7.08 us (3%)
    unnamed x4, waiting for transfers between devices  96.1 us
    all_gather x1, waiting for transfers between devices, per_device(): a_now = jax.lax.all_gather(t1, 'req', axis=0, tiled=True)  42.7 us
    psum x1, waiting for transfers between devices, per_device(): projected = lax.psum(partial_proj, 'tp')  32.4 us
    dot_general x4, matrix products, per_device(): jnp.dot(activation, down[local_block], preferred_element_type=jnp.float32)  13.6 us
    all_gather x1, blocking collectives, per_device(): all_states = lax.all_gather(states, 'tp', axis=0)  11.1 us
    all_gather x1, blocking collectives, per_device(): gathered = lax.all_gather(packed, 'tp', axis=0)  6.58 us
    dot_general x4, matrix products, per_device(): jnp.dot(rows_all, gate_up[local_block, 0], preferred_element_type=jnp.flo...  5.94 us
  transfers between devices with their start and end apart: 3, of which 3 were waited for; matrix products, arithmetic and copies ran while one was open for 0% of the time, Pallas kernels for 0%

profile of v1, /device:TPU:0, one launch (start us, length us, event | category | flops | bytes accessed | tf_op | source)
XLA Modules:
  0.0 239.1 jit_solution(13828126473498780723)
XLA Ops:
  6.6 0.8 convert_element_type.97
  7.4 0.7 reshape.253
  8.1 0.1 multiply_cosine_fusion
  8.3 0.1 subtract_convert_fusion
  8.4 0.1 pad_maximum_fusion.3
  8.5 0.7 pad_maximum_fusion.2
  9.2 6.6 %all-gather = bf16[8,24,384]{2,1,0:T(8,128)(2,1)S(1)} all-gather(bf16[2,24,384]{2,1,0:T(8,128)(2,1)S(1)} %pad_maximum_fusion.2), channel_id=2, replica_groups=mesh['req'=8,'tp'=4] {'tp'}, dimensions={0}, use_global_device_ids=true | all-gather | bytes 184320 | tf_op jit(solution)/shard_map/all_gather | solution.py:60
  16.1 0.1 reduce.1
  16.2 0.5 fusion.87
  16.9 0.5 fusion.89
  17.3 0.1 concatenate.28
  17.5 0.3 fusion.18
  17.8 0.7 fusion.17
  18.5 0.1 concatenate.29
  18.6 0.2 pad_maximum_fusion
  18.9 11.1 %all_gather.14 = f32[4,24,12,130]{3,1,2,0:T(8,128)S(1)} all-gather(f32[1,24,12,130]{3,1,2,0:T(8,128)S(1)} %pad_maximum_fusion), channel_id=1, replica_groups=mesh['req'=8,'tp'=4] {'tp'}, dimensions={0}, use_global_device_ids=true | all-gather | bytes 748800 | tf_op jit(solution)/shard_map/all_gather | solution.py:102
  30.0 0.1 subtract_convert_fusion.1
  30.1 0.1 maximum_bitcast_fusion
  30.2 0.2 fusion.71
  30.4 0.1 copy.75
  30.5 0.2 fusion.86
  30.7 0.1 copy.82
  30.8 0.1 constant_dynamic-slice_fusion.1
  30.9 0.3 copy.81
  31.3 0.6 multiply_reduce_fusion
  31.9 0.1 copy.66
  32.0 0.1 copy.83
  32.5 0.6 gather_fusion
  33.3 0.9 fusion.73
  34.3 0.1 select_reduce_fusion
  34.4 32.4 %all-reduce.3.cloned.1.call-done = f32[24,1536]{1,0:T(8,128)} async-done(((f32[24,1536]{1,0:T(8,128)}), f32[24,1536]{1,0:T(8,128)}) %all-reduce.3.cloned.1.call-update) | async-done | bytes 147472 | tf_op jit(solution)/shard_map/psum | solution.py:121
  66.8 1.0 multiply_reduce_fusion.1
  68.0 0.7 pad_maximum_fusion.1
  68.7 42.7 %all-gather.3.cloned.1.call-done = f32[192,1568]{1,0:T(8,128)} async-done(((f32[24,1568]{1,0:T(8,128)}), f32[192,1568]{1,0:T(8,128)}) %all-gather.3.cloned.1.call-update) | async-done | bytes 1204240 | tf_op jit(solution)/shard_map/all_gather | solution.py:144
  111.5 1.0 split.8
  112.5 0.4 dynamic-slice_reduce_fusion
  112.8 1.8 convolution_maximum_fusion.3
  114.6 1.4 convolution_maximum_fusion.2
  116.0 1.4 convolution_maximum_fusion.1
  117.4 1.4 convolution_maximum_fusion
  118.8 3.1 %fusion.10 = f32[192,1536]{1,0:T(8,128)} fusion(f32[192,192]{1,0:T(8,128)S(1)} %convolution_maximum_fusion.3, f32[192,1568]{1,0:T(8,128)S(1)} %copy-done.1, bf16[4,192,1536]{2,1,0:T(8,128)(2,1)} %param.23, bf16[4,2,1536,192]{2,3,1,0:T(8,128)(2,1)} %param.22, f32[192]{0:T(256)S(1)} %get-tuple-element.8), kind=kOutput, calls=%fused_computation.15 | convolution fusion | flops 227450880 | bytes 3146752 | tf_op jit(solution)/shard_map/dot_general | solution.py:152
  121.9 3.5 %fusion.8 = f32[192,1536]{1,0:T(8,128)} fusion(f32[192,1536]{1,0:T(8,128)} %fusion.10, f32[192,192]{1,0:T(8,128)S(1)} %convolution_maximum_fusion.2, f32[192,1568]{1,0:T(8,128)S(1)} %copy-done.1, bf16[4,192,1536]{2,1,0:T(8,128)(2,1)} %param.23, bf16[4,2,1536,192]{2,3,1,0:T(8,128)(2,1)} %param.22, f32[192]{0:T(256)S(1)} %get-tuple-element.7), kind=kOutput, calls=%fused_computation.12 | convolution fusion | flops 227745792 | bytes 4326400 | tf_op jit(solution)/shard_map/dot_general | solution.py:152
  125.4 3.5 %fusion.5 = f32[192,1536]{1,0:T(8,128)} fusion(f32[192,1536]{1,0:T(8,128)} %fusion.8, f32[192,192]{1,0:T(8,128)S(1)} %convolution_maximum_fusion.1, f32[192,1568]{1,0:T(8,128)S(1)} %copy-done.1, bf16[4,192,1536]{2,1,0:T(8,128)(2,1)} %param.23, bf16[4,2,1536,192]{2,3,1,0:T(8,128)(2,1)} %param.22, f32[192]{0:T(256)S(1)} %get-tuple-element.6), kind=kOutput, calls=%fused_computation.8 | convolution fusion | flops 227745792 | bytes 4326400 | tf_op jit(solution)/shard_map/dot_general | solution.py:152
  128.9 3.5 %fusion.2 = f32[192,1536]{1,0:T(8,128)} fusion(f32[192,1536]{1,0:T(8,128)} %fusion.5, f32[192,192]{1,0:T(8,128)S(1)} %convolution_maximum_fusion, f32[192,1568]{1,0:T(8,128)S(1)} %copy-done.1, bf16[4,192,1536]{2,1,0:T(8,128)(2,1)} %param.23, bf16[4,2,1536,192]{2,3,1,0:T(8,128)(2,1)} %param.22, f32[192]{0:T(256)S(1)} %get-tuple-element.5), kind=kOutput, calls=%fused_computation.4 | convolution fusion | flops 227745792 | bytes 4326400 | tf_op jit(solution)/shard_map/dot_general | solution.py:152
  132.4 1.7 reshape.250
  134.1 1.1 copy.71
  135.2 96.0 %reduce-scatter.4.cloned.1.call-done = f32[1,24,384]{2,1,0:T(8,128)} async-done(((f32[32,24,384]{2,1,0:T(8,128)}), f32[1,24,384]{2,1,0:T(8,128)}) %reduce-scatter.4.cloned.1.call-update) | async-done | bytes 36880
  231.2 1.4 fusion.70
  (52 shorter events, 1.3 us)
Async XLA Ops:
  6.5 26.7 %copy-start = (bf16[384,1536]{1,0:T(8,128)(2,1)S(1)}, bf16[384,1536]{1,0:T(8,128)(2,1)}, u32[]{:S(2)}) copy-start(bf16[384,1536]{1,0:T(8,128)(2,1)} %param.18) | copy-start | bytes 3538948
  6.5 9.4 %copy-start.7 = (s32[1,24]{1,0:T(1,128)S(1)}, s32[1,24]{1,0:T(1,128)}, u32[]{:S(2)}) copy-start(s32[1,24]{1,0:T(1,128)} %param.16) | copy-start | bytes 292
  6.5 9.7 %copy-start.2 = (bf16[768,2,2,128]{3,2,1,0:T(2,128)(2,1)S(1)}, bf16[768,2,2,128]{3,2,1,0:T(2,128)(2,1)}, u32[]{:S(2)}) copy-start(bf16[768,2,2,128]{3,2,1,0:T(2,128)(2,1)} %param.17) | copy-start | bytes 2359300
  6.5 60.3 %all-reduce.3.cloned.1.call-start = ((), (), s32[]{:S(2)}) async-start(), calls=%async_computation.1 | async-start | bytes 294912 | tf_op jit(solution)/shard_map/psum | solution.py:121
  18.5 11.4 %copy-start.3 = (bf16[24,2,256]{2,1,0:T(2,128)(2,1)S(1)}, bf16[24,2,256]{2,1,0:T(2,128)(2,1)}, u32[]{:S(2)}) copy-start(bf16[24,2,256]{2,1,0:T(2,128)(2,1)} %param.14) | copy-start | bytes 73732
  32.0 2.3 copy-start.5
  32.0 2.3 copy-start.6
  33.2 34.6 %copy-start.4 = (f32[1536]{0:T(1024)S(1)}, f32[1536]{0:T(1024)}, u32[]{:S(2)}) copy-start(f32[1536]{0:T(1024)} %param.19) | copy-start | bytes 18436
  34.2 77.2 %all-gather.3.cloned.1.call-start = ((), (), s32[]{:S(2)}) async-start(), calls=%async_computation.2 | async-start | bytes 1437696 | tf_op jit(solution)/shard_map/all_gather | solution.py:144
  68.7 162.5 %reduce-scatter.4.cloned.1.call-start = ((), (), s32[]{:S(2)}) async-start(), calls=%async_computation.3 | async-start | bytes 1216512
  111.5 3.1 %copy-start.1 = (f32[192,1568]{1,0:T(8,128)S(1)}, f32[192,1568]{1,0:T(8,128)}, u32[]{:S(2)}) copy-start(f32[192,1568]{1,0:T(8,128)} %all-gather.3.cloned.1.call-done) | copy-start | bytes 3612676
Sparse Core Ops, SparseCore 0:
  34.3 32.4 all-reduce.2
  69.0 42.4 all-gather.2
  135.3 95.8 reduce-scatter.3
